TPU v7x, 256 devices: a whole 4x4x8 slice. The times are simulated.
256 devices in a mesh: section: 2 (over core), seq: 16 (over x, y), exp: 8 (over z).
Axes of the slice: x: 4, y: 4, z: 8, core: 2. Of those that a mesh axis runs over, the one named last changes fastest.
Arguments:
- hidden_in: bfloat16 [2048, 2048], P('seq'), may hold values from -6 to 6
- seg_ids: int32 [2048], P('seq'), may hold values from 0 to 7, never falling along the last dimension, each value on 1 to 1024 neighbouring positions
- attn_gain: float32 [2048], replicated, may hold values from 0.25 to 1.75
- w_query: bfloat16 [2048, 2048], P(None, ('section', 'exp'))
- w_key: bfloat16 [2048, 2048], P(None, ('section', 'exp'))
- w_value: bfloat16 [2048, 2048], P(None, ('section', 'exp')), may hold values from -0.125 to 0.125
- w_out: bfloat16 [2048, 2048], P(('section', 'exp')), may hold values from -0.5 to 0.5
- moe_gain: float32 [2048], replicated, may hold values from 0.25 to 1.75
- expert_ids: int32 [2048, 8], P(('seq', 'exp')), may hold values from 0 to 63, all different within a row; in each aligned block of 16 rows (0 to 15, 16 to 31, ...) at most 4 rows name the same one
- route_weights: float32 [2048, 8], P(('seq', 'exp')), may hold values from 0.1 to 0.6
- gate_halves: bfloat16 [128, 2048, 512], P(('seq', 'exp'), None, 'section'), may hold values from -0.125 to 0.125
- up_halves: bfloat16 [128, 2048, 512], P(('seq', 'exp'), None, 'section'), may hold values from -0.125 to 0.125
- down_halves: bfloat16 [128, 512, 2048], P(('seq', 'exp'), 'section'), may hold values from -0.1875 to 0.1875
Outputs:
- layer_out: bfloat16 [2048, 2048], P(('seq', 'exp'))
Inputs may be any that keep to these rules, and one draw needn't show every extreme that they name: `seg_ids`: prompt numbers never fall along the batch; each prompt holds 1 to 1024 tokens, and one holds exactly 1024. `expert_ids`: A token's 8 experts are distinct. In each aligned block of 16 tokens (the tokens of one device along seq and exp), no expert is chosen by more than 4 of the block's tokens, a bound that some block reaches.
All inputs are finite; a program needn't handle non-finite values.
Results may differ from a plain program's by a relative error of at most 0.012.
Values may be sent and summed in bfloat16 or wider, within the bound.
No kernel may reach another device: no remote copies, remote signals or barrier semaphores. Data moves between devices by JAX's collectives and lax.ppermute only.
A program may use at most 64 MiB of HBM per device.

v0:
```python
import math
import jax
import jax.numpy as jnp
from jax import lax
from jax.sharding import PartitionSpec as P

epsilon = 1e-05
rope_base = 10000.0


def rms_scale(rows, gain):
    wide = rows.astype(jnp.float32)
    inverse = lax.rsqrt(jnp.mean(wide * wide, axis=-1, keepdims=True) + epsilon)
    return (wide * inverse * gain).astype(jnp.bfloat16)


def rotate(values, positions):
    half_dim = values.shape[-1] // 2
    frequency = rope_base ** (-2.0 * jnp.arange(half_dim, dtype=jnp.float32) / values.shape[-1])
    angles = positions.astype(jnp.float32)[:, None] * frequency[None, :]
    cosine = jnp.cos(angles)
    sine_part = jnp.sin(angles)
    first_half = values[:, :half_dim]
    second_half = values[:, half_dim:]
    return jnp.concatenate(
        [
            first_half * cosine - second_half * sine_part,
            second_half * cosine + first_half * sine_part,
        ],
        axis=-1,
    )


def per_device(
    hidden_in,
    seg_ids,
    attn_gain,
    w_query,
    w_key,
    w_value,
    w_out,
    moe_gain,
    expert_ids,
    route_weights,
    gate_halves,
    up_halves,
    down_halves,
):
    tok_seq = hidden_in.shape[0]
    width = hidden_in.shape[1]
    head_dim = w_query.shape[1]
    positions = lax.axis_index("seq") * tok_seq + jnp.arange(tok_seq, dtype=jnp.int32)
    normed = rms_scale(hidden_in, attn_gain)
    query_rows = rotate(
        jnp.dot(normed, w_query, preferred_element_type=jnp.float32), positions
    ).astype(jnp.bfloat16)
    key_rows = rotate(jnp.dot(normed, w_key, preferred_element_type=jnp.float32), positions).astype(
        jnp.bfloat16
    )
    value_rows = jnp.dot(normed, w_value, preferred_element_type=jnp.float32).astype(jnp.bfloat16)
    score_scale = 1.0 / math.sqrt(head_dim)
    run_max = jnp.full((tok_seq,), -1e30, jnp.float32)
    seg_block = jnp.broadcast_to(seg_ids.astype(jnp.bfloat16)[:, None], (tok_seq, head_dim))
    packed = jnp.concatenate([key_rows, value_rows, seg_block], axis=1)
    gathered = lax.all_gather(packed, "seq", axis=0, tiled=True)
    piece_keys = gathered[:, :head_dim]
    piece_values = gathered[:, head_dim : 2 * head_dim]
    key_segs = gathered[:, 2 * head_dim].astype(jnp.int32)
    piece_rows = piece_keys.shape[0]
    scores = (
        lax.dot_general(
            query_rows, piece_keys, (((1,), (1,)), ((), ())), preferred_element_type=jnp.float32
        )
        * score_scale
    )
    key_pos = jnp.arange(piece_rows, dtype=jnp.int32)
    allowed = (seg_ids[:, None] == key_segs[None, :]) & (key_pos[None, :] <= positions[:, None])
    masked = jnp.where(allowed, scores, -1e30)
    new_max = jnp.maximum(run_max, jnp.max(masked, axis=1))
    weights = jnp.where(allowed, jnp.exp(masked - new_max[:, None]), 0.0)
    run_total = jnp.sum(weights, axis=1)
    weighted_sum = jnp.dot(
        weights.astype(jnp.bfloat16), piece_values, preferred_element_type=jnp.float32
    )
    run_max, run_total, weighted_sum = (new_max, run_total, weighted_sum)
    head_out = (weighted_sum / run_total[:, None]).astype(jnp.bfloat16)
    partial_value = jnp.dot(head_out, w_out, preferred_element_type=jnp.float32)
    tok_dev = tok_seq // lax.axis_size("exp")
    own_start = lax.axis_index("exp") * tok_dev
    summed = lax.psum_scatter(partial_value, "exp", scatter_dimension=0, tiled=True)
    summed = summed + lax.ppermute(summed, "section", [(0, 1), (1, 0)])
    own_rows = lax.dynamic_slice_in_dim(hidden_in, own_start, tok_dev, 0)
    residual = (own_rows.astype(jnp.float32) + summed).astype(jnp.bfloat16)
    moe_in = rms_scale(residual, moe_gain)
    experts = lax.axis_size("seq") * lax.axis_size("exp") // 2
    top_count = expert_ids.shape[1]
    capacity = min(tok_dev, max(2, 2 * tok_dev * top_count // experts))
    row_count = tok_dev * top_count
    flat_ids = expert_ids.reshape(row_count)
    one_hot = (flat_ids[:, None] == jnp.arange(experts, dtype=jnp.int32)[None, :]).astype(jnp.int32)
    slot_rank = jnp.sum((jnp.cumsum(one_hot, axis=0) - one_hot) * one_hot, axis=1)
    slot_index = flat_ids * capacity + slot_rank
    placed = slot_index[:, None] == jnp.arange(experts * capacity, dtype=jnp.int32)[None, :]
    repeated = jnp.repeat(moe_in, top_count, axis=0)
    outgoing = lax.dot_general(
        placed.astype(jnp.bfloat16),
        repeated,
        (((0,), (0,)), ((), ())),
        preferred_element_type=jnp.float32,
    ).astype(jnp.bfloat16)
    row_token = jnp.arange(row_count, dtype=jnp.int32) // top_count
    token_hot = (row_token[None, :] == jnp.arange(tok_dev, dtype=jnp.int32)[:, None]).astype(
        jnp.float32
    )
    weighted = token_hot * route_weights.reshape(row_count)[None, :]
    combine = jnp.dot(weighted, placed.astype(jnp.float32), precision=lax.Precision.HIGHEST)
    doubled = jnp.broadcast_to(
        outgoing.reshape(experts, 1, capacity, width), (experts, 2, capacity, width)
    ).reshape(2 * experts, capacity, width)
    arrived = lax.all_to_all(doubled, ("seq", "exp"), split_axis=0, concat_axis=0, tiled=True)
    flat_rows = arrived.reshape(-1, width)
    gate_proj = jnp.dot(flat_rows, gate_halves[0], preferred_element_type=jnp.float32)
    up_proj = jnp.dot(flat_rows, up_halves[0], preferred_element_type=jnp.float32)
    activated = (jax.nn.silu(gate_proj) * up_proj).astype(jnp.bfloat16)
    returned = lax.all_to_all(
        jnp.dot(activated, down_halves[0], preferred_element_type=jnp.float32)
        .astype(jnp.bfloat16)
        .reshape(arrived.shape),
        ("seq", "exp"),
        split_axis=0,
        concat_axis=0,
        tiled=True,
    )
    halves_sum = jnp.sum(
        returned.reshape(experts, 2, capacity, width).astype(jnp.float32), axis=1
    ).reshape(experts * capacity, width)
    moe_part = jnp.dot(combine, halves_sum, precision=lax.Precision.HIGHEST)
    moe_total = moe_part + lax.ppermute(moe_part, "section", [(0, 1), (1, 0)])
    return (residual.astype(jnp.float32) + moe_total).astype(jnp.bfloat16)


def solution(mesh):
    in_specs = (
        P("seq", None),
        P("seq"),
        P(),
        P(None, ("section", "exp")),
        P(None, ("section", "exp")),
        P(None, ("section", "exp")),
        P(("section", "exp"), None),
        P(),
        P(("seq", "exp"), None),
        P(("seq", "exp"), None),
        P(("seq", "exp"), None, "section"),
        P(("seq", "exp"), None, "section"),
        P(("seq", "exp"), "section", None),
    )
    out_specs = P(("seq", "exp"), None)
    return jax.shard_map(
        per_device, mesh=mesh, in_specs=in_specs, out_specs=out_specs, check_vma=False
    )
```

profile of v0, /device:TPU:1, one launch (start us, length us, event | category | flops | bytes accessed | tf_op | source)
XLA Modules:
  0.0 270.6 jit_solution(9258952518360087763)
XLA Ops:
  6.5 0.0 copy-start
  6.5 0.0 copy-start.2
  6.5 0.0 copy-start.9
  6.5 0.0 copy-start.8
  6.5 0.0 all-gather.2.cloned.1.call-start
  6.6 0.0 copy-start.7
  6.6 1.4 fusion.4
  8.0 1.6 fusion.76
  9.6 1.6 fusion.79
  11.3 0.0 copy-done.2
  11.3 0.0 copy-done.9
  11.3 0.0 copy-done.8
  11.3 0.4 convolution_convert_fusion.2
  11.7 0.0 copy-done.7
  11.7 0.0 copy-start.3
  11.7 0.2 fusion.59
  12.0 0.6 pad_maximum_fusion
  12.6 0.0 all-gather.2.cloned.1.call-update
  12.6 0.0 reduce-scatter.2.cloned.1.call-start
  12.7 52.2 %all-gather.2.cloned.1.call-done = bf16[2048,384]{0,1:T(8,128)(2,1)} async-done(((bf16[128,384]{0,1:T(8,128)(2,1)}), bf16[2048,384]{0,1:T(8,128)(2,1)}) %all-gather.2.cloned.1.call-update) | async-done | bytes 1572880 | tf_op jit(solution)/shard_map/all_gather | solution.py:65
  64.9 0.8 slice_convert_fusion
  65.7 1.5 fusion.81
  67.2 0.5 fusion.13
  67.7 0.0 copy-done.3
  67.7 0.0 copy-start.5
  67.7 0.0 copy-start.4
  67.7 2.8 %fusion.3 = f32[128,2048]{1,0:T(8,128)} fusion(bf16[128,2048]{1,0:T(8,128)(2,1)S(1)} %copy-done.3, f32[128,2048]{1,0:T(8,128)S(1)} %get-tuple-element.14, bf16[2048,384]{0,1:T(8,128)(2,1)} %all-gather.2.cloned.1.call-done, f32[128]{0:T(128)S(1)} %broadcast_maximum_fusion, s32[128]{0:T(128)S(1)} %iota_add_fusion, s32[2048]{0:T(1024)S(1)} %bitcast.29, ...), kind=kOutput, calls=%fused_computation.12 | convolution fusion | flops 135823360 | bytes 3155968 | tf_op jit(solution)/shard_map/dot_general | solution.py:87
  70.6 0.0 reduce-scatter.2.cloned.1.call-update
  70.6 0.0 copy-done.5
  70.6 0.1 copy.17
  70.7 0.1 reshape.89
  70.8 0.1 fusion.45
  70.9 0.2 reduce_window_sum.11
  71.0 0.2 select_reduce_fusion
  71.2 35.1 %reduce-scatter.2.cloned.1.call-done = f32[16,2048]{1,0:T(8,128)} async-done(((f32[128,2048]{1,0:T(8,128)}), f32[16,2048]{1,0:T(8,128)}) %reduce-scatter.2.cloned.1.call-update) | async-done | bytes 131088 | tf_op jit(solution)/shard_map/reduce_scatter | solution.py:90
  106.3 5.2 %collective-permute-start = (f32[16,2048]{1,0:T(8,128)}, f32[16,2048]{1,0:T(8,128)S(1)}, u32[]{:S(2)}, u32[]{:S(2)}) collective-permute-start(f32[16,2048]{1,0:T(8,128)} %reduce-scatter.2.cloned.1.call-done), channel_id=1, source_target_pairs={{0,128},{128,0},{1,129},{129,1},{2,130},{130,2},{3,131},{131,3},{4... | collective-permute-start | bytes 393224 | tf_op jit(solution)/shard_map/ppermute | solution.py:91
  111.5 1.2 collective-permute-done
  112.7 1.0 fusion.38
  113.7 0.0 copy-done.4
  113.7 0.1 fusion.40
  113.8 0.5 convolution_convert_fusion.1
  114.4 0.4 broadcast_in_dim.22
  114.8 1.2 broadcast_in_dim.23
  116.0 63.8 %all_to_all.10 = bf16[128,4,2048]{2,1,0:T(4,128)(2,1)S(1)} all-to-all(bf16[128,4,2048]{2,1,0:T(4,128)(2,1)S(1)} %bitcast.26), channel_id=1, replica_groups=mesh['section'=2,'seq'=16,'exp'=8] {'seq','exp'}, dimensions={0} | all-to-all | bytes 4194304 | tf_op jit(solution)/shard_map/all_to_all | solution.py:120
  179.9 2.1 reshape.92
  181.9 0.0 copy-start.1
  181.9 3.5 %fusion.10 = f32[512,256]{1,0:T(8,128)} fusion(bf16[512,2048]{1,0:T(8,128)(2,1)} %reshape.92, bf16[1,2048,256]{2,1,0:T(8,128)(2,1)} %param.23), kind=kOutput, calls=%fused_computation.18 | convolution fusion | flops 536870912 | bytes 3670016 | tf_op jit(solution)/shard_map/dot_general | solution.py:122
  185.5 0.0 copy-done
  185.5 0.0 copy-done.1
  185.5 5.0 %convolution_convert_fusion = bf16[512,2048]{1,0:T(8,128)(2,1)} fusion(bf16[512,2048]{1,0:T(8,128)(2,1)S(1)} %copy-done.1, bf16[1,256,2048]{2,1,0:T(8,128)(2,1)S(1)} %copy-done, bf16[1,2048,256]{2,1,0:T(8,128)(2,1)} %param.24, f32[512,256]{1,0:T(8,128)} %fusion.10), kind=kOutput, calls=%fused_computation.1 | convolution fusion | flops 1075576832 | bytes 6815744 | tf_op jit(solution)/shard_map/dot_general | solution.py:126
  190.5 4.1 %reshape.93 = bf16[128,4,2048]{2,1,0:T(4,128)(2,1)} reshape(bf16[512,2048]{1,0:T(8,128)(2,1)} %convolution_convert_fusion) | data formatting | bytes 4194304 | tf_op jit(solution)/shard_map/reshape | solution.py:128
  194.6 0.0 copy-start.6
  194.6 6.5 %all-to-all-start.1 = ((bf16[128,4,2048]{2,1,0:T(4,128)(2,1)}), bf16[128,4,2048]{2,1,0:T(4,128)(2,1)S(1)}, u32[]{:S(2)}, u32[]{:S(2)}) async-start(bf16[128,4,2048]{2,1,0:T(4,128)(2,1)} %reshape.93), calls=%async_computation.2 | async-start | bytes 4194304 | tf_op jit(solution)/shard_map/all_to_all | solution.py:125
  201.1 0.0 copy-done.6
  201.1 0.1 copy.16
  201.2 0.1 mul.147
  201.3 0.2 fusion.42
  201.5 50.7 %all-to-all-done.1 = bf16[128,4,2048]{2,1,0:T(4,128)(2,1)S(1)} async-done(((bf16[128,4,2048]{2,1,0:T(4,128)(2,1)}), bf16[128,4,2048]{2,1,0:T(4,128)(2,1)S(1)}, u32[]{:S(2)}, u32[]{:S(2)}) %all-to-all-start.1) | async-done | bytes 2097184 | tf_op jit(solution)/shard_map/all_to_all | solution.py:125
  252.2 2.7 convert_reduce_fusion
  254.9 2.0 reshape.94
  256.8 1.1 fusion.82
  257.9 4.2 %collective-permute-start.1 = (f32[16,2048]{1,0:T(8,128)S(1)}, f32[16,2048]{1,0:T(8,128)S(1)}, u32[]{:S(2)}, u32[]{:S(2)}) collective-permute-start(f32[16,2048]{1,0:T(8,128)S(1)} %fusion.82), channel_id=1, source_target_pairs={{0,128},{128,0},{1,129},{129,1},{2,130},{130,2},{3,131},{131,3},{4... | collective-permute-start | bytes 393224 | tf_op jit(solution)/shard_map/ppermute | solution.py:138
  262.1 1.0 collective-permute-done.1
  263.1 0.7 fusion.41
  (10 shorter events, 0.1 us)
Async XLA Ops:
  6.5 178.9 %copy-start = (bf16[1,256,2048]{2,1,0:T(8,128)(2,1)S(1)}, bf16[1,256,2048]{2,1,0:T(8,128)(2,1)}, u32[]{:S(2)}) copy-start(bf16[1,256,2048]{2,1,0:T(8,128)(2,1)} %param.25) | copy-start | bytes 3145732
  6.5 4.7 %copy-start.2 = (bf16[128,2048]{1,0:T(8,128)(2,1)S(1)}, bf16[128,2048]{1,0:T(8,128)(2,1)}, u32[]{:S(2)}) copy-start(bf16[128,2048]{1,0:T(8,128)(2,1)} %param.13) | copy-start | bytes 1572868
  6.5 4.7 %copy-start.9 = (f32[2048]{0:T(1024)S(1)}, f32[2048]{0:T(1024)}, u32[]{:S(2)}) copy-start(f32[2048]{0:T(1024)} %param.15) | copy-start | bytes 24580
  6.5 4.7 %copy-start.8 = (bf16[2048,128]{1,0:T(8,128)(2,1)S(1)}, bf16[2048,128]{1,0:T(8,128)(2,1)}, u32[]{:S(2)}) copy-start(bf16[2048,128]{1,0:T(8,128)(2,1)} %param.18) | copy-start | bytes 1572868
  6.5 58.4 %all-gather.2.cloned.1.call-start = ((), (), s32[]{:S(2)}) async-start(), calls=%async_computation.3 | async-start | bytes 1671168 | tf_op jit(solution)/shard_map/all_gather | solution.py:65
  6.6 5.1 %copy-start.7 = (s32[128]{0:T(128)S(1)}, s32[128]{0:T(128)}, u32[]{:S(2)}) copy-start(s32[128]{0:T(128)} %param.14) | copy-start | bytes 1540
  11.7 56.0 %copy-start.3 = (bf16[128,2048]{1,0:T(8,128)(2,1)S(1)}, bf16[128,2048]{1,0:T(8,128)(2,1)}, u32[]{:S(2)}) copy-start(bf16[128,2048]{1,0:T(8,128)(2,1)} %param.19) | copy-start | bytes 1572868
  12.6 93.7 %reduce-scatter.2.cloned.1.call-start = ((), (), s32[]{:S(2)}) async-start(), calls=%async_computation.4 | async-start | bytes 1179648 | tf_op jit(solution)/shard_map/reduce_scatter | solution.py:90
  67.7 2.9 %copy-start.5 = (s32[16,8]{0,1:T(8,128)S(1)}, s32[16,8]{0,1:T(8,128)}, u32[]{:S(2)}) copy-start(s32[16,8]{0,1:T(8,128)} %param.21) | copy-start | bytes 1540
  67.7 46.0 %copy-start.4 = (f32[2048]{0:T(1024)S(1)}, f32[2048]{0:T(1024)}, u32[]{:S(2)}) copy-start(f32[2048]{0:T(1024)} %param.20) | copy-start | bytes 24580
  106.3 6.4 %collective-permute-start = (f32[16,2048]{1,0:T(8,128)}, f32[16,2048]{1,0:T(8,128)S(1)}, u32[]{:S(2)}, u32[]{:S(2)}) collective-permute-start(f32[16,2048]{1,0:T(8,128)} %reduce-scatter.2.cloned.1.call-done), channel_id=1, source_target_pairs={{0,128},{128,0},{1,129},{129,1},{2,130},{130,2},{3,131},{131,3},{4... | collective-permute-start | bytes 393224 | tf_op jit(solution)/shard_map/ppermute | solution.py:91
  181.9 3.5 %copy-start.1 = (bf16[512,2048]{1,0:T(8,128)(2,1)S(1)}, bf16[512,2048]{1,0:T(8,128)(2,1)}, u32[]{:S(2)}) copy-start(bf16[512,2048]{1,0:T(8,128)(2,1)} %reshape.92) | copy-start | bytes 6291460
  194.6 6.5 %copy-start.6 = (f32[16,8]{0,1:T(8,128)S(1)}, f32[16,8]{0,1:T(8,128)}, u32[]{:S(2)}) copy-start(f32[16,8]{0,1:T(8,128)} %param.22) | copy-start | bytes 1540
  194.6 57.6 %all-to-all-start.1 = ((bf16[128,4,2048]{2,1,0:T(4,128)(2,1)}), bf16[128,4,2048]{2,1,0:T(4,128)(2,1)S(1)}, u32[]{:S(2)}, u32[]{:S(2)}) async-start(bf16[128,4,2048]{2,1,0:T(4,128)(2,1)} %reshape.93), calls=%async_computation.2 | async-start | bytes 4194304 | tf_op jit(solution)/shard_map/all_to_all | solution.py:125
  257.9 5.2 %collective-permute-start.1 = (f32[16,2048]{1,0:T(8,128)S(1)}, f32[16,2048]{1,0:T(8,128)S(1)}, u32[]{:S(2)}, u32[]{:S(2)}) collective-permute-start(f32[16,2048]{1,0:T(8,128)S(1)} %fusion.82), channel_id=1, source_target_pairs={{0,128},{128,0},{1,129},{129,1},{2,130},{130,2},{3,131},{131,3},{4... | collective-permute-start | bytes 393224 | tf_op jit(solution)/shard_map/ppermute | solution.py:138
Sparse Core Ops, SparseCore 0:
  12.7 52.1 all-gather.1
  70.7 35.5 reduce-scatter.1
where the time goes:
time: 271 us
  waiting for transfers between devices  140 us (52%)
  blocking collectives  63.8 us (24%)
  matrix products  18.4 us (7%)
  starting transfers between devices  16 us (6%)
  between operations  13.7 us (5%)
  local copies, waits for them, and re-layouts  10.2 us (4%)
  other arithmetic  8.38 us (3%)
    all_to_all x1, blocking collectives, per_device(): lax.all_to_all(doubled, ('seq', 'exp'), split_axis=0, concat_axis=0, tile...  63.8 us
    all_gather x1, waiting for transfers between devices, per_device(): gathered = lax.all_gather(packed, 'seq', axis=0, tiled=True)  52.2 us
    all_to_all x1, waiting for transfers between devices, per_device(): lax.all_to_all(jnp.dot(activated, down_halves[0], preferred_element_type=...  50.7 us
    reduce_scatter x1, waiting for transfers between devices, per_device(): lax.psum_scatter(partial_value, 'exp', scatter_dimension=0, tiled=True)  35.1 us
    all_to_all x1, starting transfers between devices, per_device(): lax.all_to_all(jnp.dot(activated, down_halves[0], preferred_element_type=...  6.52 us
  transfers between devices with their start and end apart: 5, of which 5 were waited for; matrix products, arithmetic and copies ran while one was open for 0% of the time, Pallas kernels for 0%

commit v1 on v0

--- a/solution.py
+++ b/solution.py
@@ -62,7 +62,9 @@
     run_max = jnp.full((tok_seq,), -1e30, jnp.float32)
     seg_block = jnp.broadcast_to(seg_ids.astype(jnp.bfloat16)[:, None], (tok_seq, head_dim))
     packed = jnp.concatenate([key_rows, value_rows, seg_block], axis=1)
-    gathered = lax.all_gather(packed, "seq", axis=0, tiled=True)
+    gathered = jnp.concatenate(
+        lax.all_to_all(jnp.stack([packed] * lax.psum(1, "seq")), "seq", 0, 0), axis=0
+    )
     piece_keys = gathered[:, :head_dim]
     piece_values = gathered[:, head_dim : 2 * head_dim]
     key_segs = gathered[:, 2 * head_dim].astype(jnp.int32)

time: 271 us -> 253 us (0.934)
  waiting for transfers between devices: 140 us -> 110 us
  starting transfers between devices: 16 us -> 24 us
  local copies, waits for them, and re-layouts: 10.2 us -> 13.2 us
    all_gather x1 -> x0, waiting for transfers between devices: 52.2 us -> none  [per_device(): gathered = lax.all_gather(packed, 'seq', axis=0, tiled=True)]
    all_to_all x0 -> x1, waiting for transfers between devices: none -> 20.7 us  [per_device(): lax.all_to_all(jnp.stack([packed] * lax.psum(1, 'seq')), 'seq', 0, 0)]
    all_to_all x0 -> x1, starting transfers between devices: none -> 7.58 us  [per_device(): lax.all_to_all(jnp.stack([packed] * lax.psum(1, 'seq')), 'seq', 0, 0)]
where the time goes in v1:
time: 253 us; the launch traced here: 252 us
  waiting for transfers between devices  110 us (43%)
  blocking collectives  63.9 us (25%)
  starting transfers between devices  24 us (9%)
  matrix products  18.3 us (7%)
  between operations  13.7 us (5%)
  local copies, waits for them, and re-layouts  13.2 us (5%)
  other arithmetic  8.46 us (3%)
    all_to_all x1, blocking collectives, per_device(): lax.all_to_all(doubled, ('seq', 'exp'), split_axis=0, concat_axis=0, tile...  63.9 us
    all_to_all x1, waiting for transfers between devices, per_device(): lax.all_to_all(jnp.dot(activated, down_halves[0], preferred_element_type=...  50.8 us
    reduce_scatter x1, waiting for transfers between devices, per_device(): lax.psum_scatter(partial_value, 'exp', scatter_dimension=0, tiled=True)  36.7 us
    all_to_all x1, waiting for transfers between devices, per_device(): lax.all_to_all(jnp.stack([packed] * lax.psum(1, 'seq')), 'seq', 0, 0)  20.7 us
    all_to_all x1, starting transfers between devices, per_device(): lax.all_to_all(jnp.stack([packed] * lax.psum(1, 'seq')), 'seq', 0, 0)  7.58 us
    all_to_all x1, starting transfers between devices, per_device(): lax.all_to_all(jnp.dot(activated, down_halves[0], preferred_element_type=...  6.52 us
    ppermute x1, starting transfers between devices, per_device(): summed = summed + lax.ppermute(summed, 'section', [(0, 1), (1, 0)])  5.63 us
  transfers between devices with their start and end apart: 5, of which 5 were waited for; matrix products, arithmetic and copies ran while one was open for 0% of the time, Pallas kernels for 0%

profile of v1, /device:TPU:1, one launch (start us, length us, event | category | flops | bytes accessed | tf_op | source)
XLA Modules:
  0.0 251.9 jit_solution(10548553380876669806)
XLA Ops:
  6.5 0.0 copy-start
  6.5 0.0 copy-start.2
  6.5 0.0 copy-start.9
  6.5 0.0 copy-start.8
  6.6 0.0 copy-start.7
  6.6 1.4 fusion.4
  7.9 1.6 fusion.76
  9.6 1.6 fusion.79
  11.2 0.0 copy-done.2
  11.2 0.0 copy-done.9
  11.2 0.0 copy-done.8
  11.3 0.4 convolution_convert_fusion.2
  11.7 0.0 copy-done.7
  11.7 0.2 fusion.59
  11.9 1.5 stack.2
  13.4 7.6 %all-to-all-start = ((bf16[16,128,384]{1,2,0:T(8,128)(2,1)}), bf16[16,128,384]{1,2,0:T(8,128)(2,1)S(1)}, u32[]{:S(2)}, u32[]{:S(2)}) async-start(bf16[16,128,384]{1,2,0:T(8,128)(2,1)} %stack.2), calls=%async_computation | async-start | bytes 3145728 | tf_op jit(solution)/shard_map/all_to_all | solution.py:66
  21.0 0.0 reduce-scatter.2.cloned.1.call-start
  21.0 20.7 %all-to-all-done = bf16[16,128,384]{1,2,0:T(8,128)(2,1)S(1)} async-done(((bf16[16,128,384]{1,2,0:T(8,128)(2,1)}), bf16[16,128,384]{1,2,0:T(8,128)(2,1)S(1)}, u32[]{:S(2)}, u32[]{:S(2)}) %all-to-all-start) | async-done | bytes 1572896 | tf_op jit(solution)/shard_map/all_to_all | solution.py:66
  41.7 1.6 copy.21
  43.3 0.0 copy-start.3
  43.3 1.4 convert_reduce_fusion.1
  44.7 1.6 fusion.81
  46.3 0.5 fusion.13
  46.8 0.0 copy-done.3
  46.8 0.0 copy-start.5
  46.8 0.0 copy-start.4
  46.8 2.7 %fusion.3 = f32[128,2048]{1,0:T(8,128)} fusion(bf16[128,2048]{1,0:T(8,128)(2,1)S(1)} %copy-done.3, f32[128,2048]{1,0:T(8,128)S(1)} %get-tuple-element.14, bf16[2048,384]{1,0:T(8,128)(2,1)} %bitcast.29, f32[128]{0:T(128)S(1)} %broadcast_maximum_fusion, s32[128]{0:T(128)S(1)} %iota_add_fusion, s32[2048]{0:T(1024)S(1)} %convert_reduce_fusion.1, ...), kind=kOutput, calls=%fused_computation.12 | convolution fusion | flops 135823360 | bytes 3155968 | tf_op jit(solution)/shard_map/dot_general | solution.py:89
  49.5 0.0 reduce-scatter.2.cloned.1.call-update
  49.5 0.0 copy-done.5
  49.5 0.1 copy.23
  49.6 0.1 reshape.95
  49.7 0.1 fusion.45
  49.8 0.2 reduce_window_sum.11
  50.0 0.2 select_reduce_fusion
  50.2 36.7 %reduce-scatter.2.cloned.1.call-done = f32[16,2048]{1,0:T(8,128)} async-done(((f32[128,2048]{1,0:T(8,128)}), f32[16,2048]{1,0:T(8,128)}) %reduce-scatter.2.cloned.1.call-update) | async-done | bytes 131088 | tf_op jit(solution)/shard_map/reduce_scatter | solution.py:92
  86.9 5.6 %collective-permute-start = (f32[16,2048]{1,0:T(8,128)}, f32[16,2048]{1,0:T(8,128)S(1)}, u32[]{:S(2)}, u32[]{:S(2)}) collective-permute-start(f32[16,2048]{1,0:T(8,128)} %reduce-scatter.2.cloned.1.call-done), channel_id=1, source_target_pairs={{0,128},{128,0},{1,129},{129,1},{2,130},{130,2},{3,131},{131,3},{4... | collective-permute-start | bytes 393224 | tf_op jit(solution)/shard_map/ppermute | solution.py:93
  92.5 1.2 collective-permute-done
  93.7 1.1 fusion.38
  94.8 0.0 copy-done.4
  94.8 0.1 fusion.40
  94.9 0.5 convolution_convert_fusion.1
  95.4 0.4 broadcast_in_dim.22
  95.8 1.2 broadcast_in_dim.23
  97.1 63.9 %all_to_all.15 = bf16[128,4,2048]{2,1,0:T(4,128)(2,1)S(1)} all-to-all(bf16[128,4,2048]{2,1,0:T(4,128)(2,1)S(1)} %bitcast.26), channel_id=1, replica_groups=mesh['section'=2,'seq'=16,'exp'=8] {'seq','exp'}, dimensions={0} | all-to-all | bytes 4194304 | tf_op jit(solution)/shard_map/all_to_all | solution.py:122
  161.0 2.1 reshape.98
  163.1 0.0 copy-start.1
  163.1 3.5 %fusion.10 = f32[512,256]{1,0:T(8,128)} fusion(bf16[512,2048]{1,0:T(8,128)(2,1)} %reshape.98, bf16[1,2048,256]{2,1,0:T(8,128)(2,1)} %param.23), kind=kOutput, calls=%fused_computation.18 | convolution fusion | flops 536870912 | bytes 3670016 | tf_op jit(solution)/shard_map/dot_general | solution.py:124
  166.6 0.0 copy-done
  166.6 0.0 copy-done.1
  166.6 5.0 %convolution_convert_fusion = bf16[512,2048]{1,0:T(8,128)(2,1)} fusion(bf16[512,2048]{1,0:T(8,128)(2,1)S(1)} %copy-done.1, bf16[1,256,2048]{2,1,0:T(8,128)(2,1)S(1)} %copy-done, bf16[1,2048,256]{2,1,0:T(8,128)(2,1)} %param.24, f32[512,256]{1,0:T(8,128)} %fusion.10), kind=kOutput, calls=%fused_computation.1 | convolution fusion | flops 1075576832 | bytes 6815744 | tf_op jit(solution)/shard_map/dot_general | solution.py:128
  171.6 4.1 %reshape.99 = bf16[128,4,2048]{2,1,0:T(4,128)(2,1)} reshape(bf16[512,2048]{1,0:T(8,128)(2,1)} %convolution_convert_fusion) | data formatting | bytes 4194304 | tf_op jit(solution)/shard_map/reshape | solution.py:130
  175.7 0.0 copy-start.6
  175.7 6.5 %all-to-all-start.2 = ((bf16[128,4,2048]{2,1,0:T(4,128)(2,1)}), bf16[128,4,2048]{2,1,0:T(4,128)(2,1)S(1)}, u32[]{:S(2)}, u32[]{:S(2)}) async-start(bf16[128,4,2048]{2,1,0:T(4,128)(2,1)} %reshape.99), calls=%async_computation.3 | async-start | bytes 4194304 | tf_op jit(solution)/shard_map/all_to_all | solution.py:127
  182.2 0.0 copy-done.6
  182.3 0.1 copy.22
  182.3 0.1 mul.147
  182.4 0.2 fusion.42
  182.6 50.8 %all-to-all-done.2 = bf16[128,4,2048]{2,1,0:T(4,128)(2,1)S(1)} async-done(((bf16[128,4,2048]{2,1,0:T(4,128)(2,1)}), bf16[128,4,2048]{2,1,0:T(4,128)(2,1)S(1)}, u32[]{:S(2)}, u32[]{:S(2)}) %all-to-all-start.2) | async-done | bytes 2097184 | tf_op jit(solution)/shard_map/all_to_all | solution.py:127
  233.5 2.7 %convert_reduce_fusion = f32[64,4,2048]{2,1,0:T(4,128)} fusion(bf16[128,4,2048]{2,1,0:T(4,128)(2,1)S(1)} %all-to-all-done.2), kind=kLoop, calls=%fused_computation | loop fusion | flops 1572864 | bytes 4194304 | tf_op jit(solution)/shard_map/reduce_sum | solution.py:136
  236.2 2.0 reshape.100
  238.1 1.1 fusion.82
  239.2 4.2 %collective-permute-start.1 = (f32[16,2048]{1,0:T(8,128)S(1)}, f32[16,2048]{1,0:T(8,128)S(1)}, u32[]{:S(2)}, u32[]{:S(2)}) collective-permute-start(f32[16,2048]{1,0:T(8,128)S(1)} %fusion.82), channel_id=1, source_target_pairs={{0,128},{128,0},{1,129},{129,1},{2,130},{130,2},{3,131},{131,3},{4... | collective-permute-start | bytes 393224 | tf_op jit(solution)/shard_map/ppermute | solution.py:140
  243.4 1.0 collective-permute-done.1
  244.4 0.7 fusion.41
  (11 shorter events, 0.1 us)
Async XLA Ops:
  6.5 160.0 %copy-start = (bf16[1,256,2048]{2,1,0:T(8,128)(2,1)S(1)}, bf16[1,256,2048]{2,1,0:T(8,128)(2,1)}, u32[]{:S(2)}) copy-start(bf16[1,256,2048]{2,1,0:T(8,128)(2,1)} %param.25) | copy-start | bytes 3145732
  6.5 4.7 %copy-start.2 = (bf16[128,2048]{1,0:T(8,128)(2,1)S(1)}, bf16[128,2048]{1,0:T(8,128)(2,1)}, u32[]{:S(2)}) copy-start(bf16[128,2048]{1,0:T(8,128)(2,1)} %param.13) | copy-start | bytes 1572868
  6.5 4.7 %copy-start.9 = (f32[2048]{0:T(1024)S(1)}, f32[2048]{0:T(1024)}, u32[]{:S(2)}) copy-start(f32[2048]{0:T(1024)} %param.15) | copy-start | bytes 24580
  6.5 4.7 %copy-start.8 = (bf16[2048,128]{1,0:T(8,128)(2,1)S(1)}, bf16[2048,128]{1,0:T(8,128)(2,1)}, u32[]{:S(2)}) copy-start(bf16[2048,128]{1,0:T(8,128)(2,1)} %param.18) | copy-start | bytes 1572868
  6.6 5.1 %copy-start.7 = (s32[128]{0:T(128)S(1)}, s32[128]{0:T(128)}, u32[]{:S(2)}) copy-start(s32[128]{0:T(128)} %param.14) | copy-start | bytes 1540
  13.4 28.3 %all-to-all-start = ((bf16[16,128,384]{1,2,0:T(8,128)(2,1)}), bf16[16,128,384]{1,2,0:T(8,128)(2,1)S(1)}, u32[]{:S(2)}, u32[]{:S(2)}) async-start(bf16[16,128,384]{1,2,0:T(8,128)(2,1)} %stack.2), calls=%async_computation | async-start | bytes 3145728 | tf_op jit(solution)/shard_map/all_to_all | solution.py:66
  21.0 65.9 %reduce-scatter.2.cloned.1.call-start = ((), (), s32[]{:S(2)}) async-start(), calls=%async_computation.4 | async-start | bytes 1179648 | tf_op jit(solution)/shard_map/reduce_scatter | solution.py:92
  43.3 3.5 %copy-start.3 = (bf16[128,2048]{1,0:T(8,128)(2,1)S(1)}, bf16[128,2048]{1,0:T(8,128)(2,1)}, u32[]{:S(2)}) copy-start(bf16[128,2048]{1,0:T(8,128)(2,1)} %param.19) | copy-start | bytes 1572868
  46.8 2.8 %copy-start.5 = (s32[16,8]{0,1:T(8,128)S(1)}, s32[16,8]{0,1:T(8,128)}, u32[]{:S(2)}) copy-start(s32[16,8]{0,1:T(8,128)} %param.21) | copy-start | bytes 1540
  46.8 48.0 %copy-start.4 = (f32[2048]{0:T(1024)S(1)}, f32[2048]{0:T(1024)}, u32[]{:S(2)}) copy-start(f32[2048]{0:T(1024)} %param.20) | copy-start | bytes 24580
  86.9 6.8 %collective-permute-start = (f32[16,2048]{1,0:T(8,128)}, f32[16,2048]{1,0:T(8,128)S(1)}, u32[]{:S(2)}, u32[]{:S(2)}) collective-permute-start(f32[16,2048]{1,0:T(8,128)} %reduce-scatter.2.cloned.1.call-done), channel_id=1, source_target_pairs={{0,128},{128,0},{1,129},{129,1},{2,130},{130,2},{3,131},{131,3},{4... | collective-permute-start | bytes 393224 | tf_op jit(solution)/shard_map/ppermute | solution.py:93
  163.1 3.5 %copy-start.1 = (bf16[512,2048]{1,0:T(8,128)(2,1)S(1)}, bf16[512,2048]{1,0:T(8,128)(2,1)}, u32[]{:S(2)}) copy-start(bf16[512,2048]{1,0:T(8,128)(2,1)} %reshape.98) | copy-start | bytes 6291460
  175.7 6.5 %copy-start.6 = (f32[16,8]{0,1:T(8,128)S(1)}, f32[16,8]{0,1:T(8,128)}, u32[]{:S(2)}) copy-start(f32[16,8]{0,1:T(8,128)} %param.22) | copy-start | bytes 1540
  175.7 57.8 %all-to-all-start.2 = ((bf16[128,4,2048]{2,1,0:T(4,128)(2,1)}), bf16[128,4,2048]{2,1,0:T(4,128)(2,1)S(1)}, u32[]{:S(2)}, u32[]{:S(2)}) async-start(bf16[128,4,2048]{2,1,0:T(4,128)(2,1)} %reshape.99), calls=%async_computation.3 | async-start | bytes 4194304 | tf_op jit(solution)/shard_map/all_to_all | solution.py:127
  239.2 5.2 %collective-permute-start.1 = (f32[16,2048]{1,0:T(8,128)S(1)}, f32[16,2048]{1,0:T(8,128)S(1)}, u32[]{:S(2)}, u32[]{:S(2)}) collective-permute-start(f32[16,2048]{1,0:T(8,128)S(1)} %fusion.82), channel_id=1, source_target_pairs={{0,128},{128,0},{1,129},{129,1},{2,130},{130,2},{3,131},{131,3},{4... | collective-permute-start | bytes 393224 | tf_op jit(solution)/shard_map/ppermute | solution.py:140
Sparse Core Ops, SparseCore 0:
  49.7 37.1 reduce-scatter.1
